TPU v7x, 256 devices: a whole 4x4x8 slice. The times are simulated.
256 devices in a mesh: line: 8 (over x, core), grp: 32 (over y, z).
Axes of the slice: x: 4, y: 4, z: 8, core: 2. Of those that a mesh axis runs over, the one named last changes fastest.
Arguments:
- shot_traces: float32 [512, 192, 4096], P(('line', 'grp')), may hold values from -6 to 6
- aperture: int32 [256, 3, 32, 16], replicated, may hold values from -1 to 95, as said below
- taper_index: int32 [256, 3, 32, 16], P(('line', 'grp')), may hold values from 0 to 7
- taper_table: float32 [8, 2], replicated, may hold values from 0.2 to 1
Outputs:
- multiples: float32 [512, 192, 2, 128], P(('line', 'grp'))
Inputs may be any that keep to these rules, and one draw needn't show every extreme that they name: `aperture`: each entry is -1 for an empty slot, or r = q * 32 + h with q - s between -1 and 1, s being the entry's second index.
All inputs are finite; a program needn't handle non-finite values.
Results may differ from a plain program's by a relative error of at most 0.0003.
Values sent between devices are 32-bit elements; how exact they have to be, the bound alone decides.
No kernel may reach another device: no remote copies, remote signals or barrier semaphores. Data moves between devices by JAX's collectives and lax.ppermute only.
A program may use at most 128 MiB of HBM per device.

v0:
```python
import math

import jax
import jax.numpy as jnp
from jax import lax
from jax.sharding import PartitionSpec as P

NF = 128
BP = 2
CAP = 16
RADIX = 64

HIGHEST = lax.Precision.HIGHEST


def dft_matrix(samples):
    inner = samples // RADIX
    major = jnp.arange(RADIX, dtype=jnp.int32)
    minor = jnp.arange(inner, dtype=jnp.int32)
    bins = jnp.arange(NF, dtype=jnp.int32)
    step = 2.0 * math.pi / samples
    angle_a = ((major[:, None] * inner * bins[None, :]) % samples).astype(jnp.float32) * step
    angle_n = ((minor[:, None] * bins[None, :]) % samples).astype(jnp.float32) * step
    a_re, a_im = jnp.cos(angle_a), -jnp.sin(angle_a)
    n_re, n_im = jnp.cos(angle_n), -jnp.sin(angle_n)
    scale = 1.0 / math.sqrt(samples)
    c_re = (a_re[:, None, :] * n_re[None, :, :] - a_im[:, None, :] * n_im[None, :, :]) * scale
    c_im = (a_re[:, None, :] * n_im[None, :, :] + a_im[:, None, :] * n_re[None, :, :]) * scale
    return jnp.concatenate([c_re, c_im], axis=-1).reshape(samples, 2 * NF)


def spectrum(traces, table):
    shots, recv, samples = traces.shape
    out = jnp.dot(traces.reshape(shots * recv, samples), table, precision=HIGHEST)
    return out.reshape(shots, recv // BP, BP, 2, NF)


def combine(side_cols, weight, gathered):
    scaled = gathered * jnp.transpose(weight, (0, 2, 1))[:, :, :, None, None, None]
    col_re = side_cols[:, :, :, None, None, 0, :]
    col_im = side_cols[:, :, :, None, None, 1, :]
    row_re = scaled[None, :, :, :, :, 0, :]
    row_im = scaled[None, :, :, :, :, 1, :]
    prod_re = -jnp.sum(col_re * row_re - col_im * row_im, axis=(1, 2))
    prod_im = -jnp.sum(col_re * row_im + col_im * row_re, axis=(1, 2))
    return jnp.stack([prod_re, prod_im], axis=3)


def body(shot_traces, aperture, taper_index, taper_table):
    group_count = lax.axis_size("grp")
    line_count = lax.axis_size("line")
    my_line = lax.axis_index("line")
    my_group = lax.axis_index("grp")
    shots, recv, samples = shot_traces.shape
    sides = 3
    width = recv // (BP * sides)
    blocks = sides * width
    up = [(i, (i + 1) % line_count) for i in range(line_count)]
    down = [((i + 1) % line_count, i) for i in range(line_count)]

    tapers = lax.all_gather(taper_index.reshape(sides, group_count, CAP), "grp", axis=0, tiled=False)
    tapers = lax.dynamic_index_in_dim(tapers, my_group, 2, False)
    full_table = aperture.reshape(line_count, group_count, sides, group_count, CAP)
    slot_list = lax.dynamic_index_in_dim(
        lax.dynamic_index_in_dim(full_table, my_line, 0, False), my_group, 2, False
    )
    taper_rows = taper_table.shape[0]
    pick = tapers[..., None] == jnp.arange(taper_rows, dtype=jnp.int32)
    slot_weight = jnp.sum(
        jnp.where(pick[..., None], taper_table[None, None, None, :, :], 0.0), axis=3
    )
    hit = slot_list[..., None] == jnp.arange(blocks, dtype=jnp.int32)
    weight = jnp.sum(
        jnp.where(hit[..., None], slot_weight[:, :, :, None, :], 0.0), axis=2
    )

    table = dft_matrix(samples)
    thirds = [
        spectrum(lax.slice_in_dim(shot_traces, q * width * BP, (q + 1) * width * BP, axis=1), table)
        for q in range(sides)
    ]
    side_cols = [
        lax.ppermute(thirds[2], "line", up),
        thirds[1],
        lax.ppermute(thirds[0], "line", down),
    ]
    gathered = [lax.all_gather(t, "grp", axis=0, tiled=False) for t in thirds]

    parts = {}
    for q in range(sides):
        for s in range(sides):
            if not 0 <= q + 1 - s < sides:
                continue
            w = weight[:, s, q * width:(q + 1) * width, :]
            parts[s, q] = combine(side_cols[s], w, gathered[q])

    to_down = jnp.concatenate([parts[0, 0], parts[0, 1]], axis=1)
    to_up = jnp.concatenate([parts[2, 1], parts[2, 2]], axis=1)
    from_up = lax.ppermute(to_down, "line", down)
    from_down = lax.ppermute(to_up, "line", up)
    local = jnp.concatenate([parts[1, q] for q in range(sides)], axis=1)
    result = local
    result = result.at[:, width:].add(from_up)
    result = result.at[:, : 2 * width].add(from_down)
    return result.reshape(shots, recv, 2, NF)


def solution(mesh):
    return jax.shard_map(
        body,
        mesh=mesh,
        in_specs=(P(("line", "grp"), None, None), P(), P(("line", "grp"), None, None, None), P()),
        out_specs=P(("line", "grp"), None, None, None),
        check_vma=False,
    )
```

profile of v0, /device:TPU:32, one launch (start us, length us, event | category | flops | bytes accessed | tf_op | source)
XLA Modules:
  0.0 293.1 jit_solution(3904123376795424607)
XLA Ops:
  6.9 5.4 %fusion.25 = (f32[2,64,4096]{2,1,0:T(8,128)}, f32[2,64,4096]{2,1,0:T(8,128)S(1)}, f32[2,64,4096]{2,1,0:T(8,128)}) fusion(f32[2,192,4096]{2,1,0:T(8,128)} %param.8), kind=kLoop, calls=%fused_computation.104 | loop fusion | bytes 12582912 | tf_op jit(solution)/shard_map/slice | solution.py:79
  12.9 1.3 copy-done
  14.2 6.8 %fusion.3 = f32[128,256]{0,1:T(8,128)S(1)} fusion(f32[128,4096]{1,0:T(8,128)S(1)} %bitcast.119, f32[4096,128]{1,0:T(8,128)S(1)} %bitcast.114, f32[4096,128]{1,0:T(8,128)S(1)} %bitcast.111), kind=kOutput, calls=%fused_computation.42 | convolution fusion | flops 1611661312 | bytes 6422528 | tf_op jit(solution)/shard_map/dot_general | solution.py:34
  21.2 0.7 copy.92
  22.1 8.9 %fusion.5 = f32[128,256]{0,1:T(8,128)S(1)} fusion(f32[128,4096]{1,0:T(8,128)} %bitcast.118, f32[4096,128]{1,0:T(8,128)} %bitcast.115, f32[4096,128]{1,0:T(8,128)S(1)} %bitcast.112), kind=kOutput, calls=%fused_computation.44 | convolution fusion | flops 1611661312 | bytes 6422528 | tf_op jit(solution)/shard_map/dot_general | solution.py:34
  31.2 0.7 copy.94
  32.1 8.9 %fusion.4 = f32[128,256]{0,1:T(8,128)S(1)} fusion(f32[128,4096]{1,0:T(8,128)} %bitcast.117, f32[4096,128]{1,0:T(8,128)} %bitcast.116, f32[4096,128]{1,0:T(8,128)S(1)} %bitcast.113), kind=kOutput, calls=%fused_computation.43 | convolution fusion | flops 1611661312 | bytes 6422528 | tf_op jit(solution)/shard_map/dot_general | solution.py:34
  41.2 0.7 copy.87
  42.0 2.2 collective-permute-start.2
  44.4 5.1 %reshape.371 = s32[8,32,3,32,16]{1,0,4,3,2:T(8,128)} reshape(s32[256,3,32,16]{0,3,2,1:T(8,128)} %param.9) | data formatting | bytes 3145728 | tf_op jit(solution)/shard_map/reshape | solution.py:63
  49.4 0.9 constant_dynamic-slice_fusion.1
  50.5 53.4 %all_gather.13 = s32[32,3,32,16]{2,3,1,0:T(8,128)S(1)} all-gather(s32[1,3,32,16]{2,3,1,0:T(8,128)S(1)} %copy-done.6), channel_id=1, replica_groups=mesh['line'=8,'grp'=32] {'grp'}, dimensions={0}, use_global_device_ids=true | all-gather | bytes 202752 | tf_op jit(solution)/shard_map/all_gather | solution.py:61
  105.3 0.8 select_reduce_fusion
  106.6 1.4 all-gather.6.cloned.1.call-done
  108.0 5.8 %broadcast_multiply_fusion.1 = (f32[32,2,32,2,2,128]{5,2,4,3,1,0:T(8,128)S(1)}, f32[32,2,32,2,2,128]{5,2,4,3,1,0:T(8,128)}, f32[32,2,32,2,2,128]{5,2,4,3,1,0:T(8,128)}) fusion(f32[32,2,32,2,2,128]{5,2,4,3,1,0:T(8,128)} %all-gather.6.cloned.1.call-done, f32[32,2,32]{2,1,0:T(2,128)S(1)} %get-tuple-element.84, f32[32,2,32]{2,1,0:T(2,128)S(1)} %get-tuple-element.85, ...), kind=kLoop, calls=%fused_computation.33 | loop fusion | flops 3145728 | bytes 16801792 | tf_op jit(solution)/shard_map/mul | solution.py:39
  113.8 1.8 slice_bitcast_fusion.3
  115.6 74.1 %all-gather.8.cloned.1.call-done = f32[32,2,32,2,2,128]{5,2,4,3,1,0:T(8,128)} async-done(((f32[1,2,32,2,2,128]{5,2,4,3,1,0:T(8,128)}), f32[32,2,32,2,2,128]{5,2,4,3,1,0:T(8,128)}) %all-gather.8.cloned.1.call-update) | async-done | bytes 4194320 | tf_op jit(solution)/shard_map/all_gather | solution.py:87
  189.7 4.3 %broadcast_multiply_fusion = (f32[32,2,32,2,2,128]{5,2,4,3,1,0:T(8,128)S(1)}, f32[32,2,32,2,2,128]{5,2,4,3,1,0:T(8,128)}) fusion(f32[32,2,32,2,2,128]{5,2,4,3,1,0:T(8,128)} %all-gather.8.cloned.1.call-done, f32[32,2,32]{2,1,0:T(2,128)S(1)} %get-tuple-element.83, f32[32,2,32]{2,1,0:T(2,128)S(1)} %get-tuple-element.87), kind=kLoop, calls=%fused_computation.32 | loop fusion | flops 2097152 | bytes 12599296 | tf_op jit(solution)/shard_map/mul | solution.py:39
  194.0 0.6 slice_bitcast_fusion
  194.6 0.9 copy-done.5
  195.6 2.3 subtract_reduce_fusion.1
  198.0 1.8 slice_bitcast_fusion.4
  199.8 71.1 %all-gather.4.cloned.1.call-done = f32[32,2,32,2,2,128]{5,2,4,3,1,0:T(8,128)} async-done(((f32[1,2,32,2,2,128]{5,2,4,3,1,0:T(8,128)}), f32[32,2,32,2,2,128]{5,2,4,3,1,0:T(8,128)}) %all-gather.4.cloned.1.call-update) | async-done | bytes 4194320 | tf_op jit(solution)/shard_map/all_gather | solution.py:87
  270.9 3.0 %broadcast_multiply_fusion.3 = (f32[32,2,32,2,2,128]{5,2,4,3,1,0:T(8,128)S(1)}, f32[32,2,32,2,2,128]{5,2,4,3,1,0:T(8,128)S(1)}) fusion(f32[32,2,32,2,2,128]{5,2,4,3,1,0:T(8,128)} %all-gather.4.cloned.1.call-done, f32[32,2,32]{2,1,0:T(2,128)S(1)} %get-tuple-element.86, f32[32,2,32]{2,1,0:T(2,128)S(1)} %get-tuple-element.89), kind=kLoop, calls=%fused_computation.35 | loop fusion | flops 2097152 | bytes 12599296 | tf_op jit(solution)/shard_map/mul | solution.py:39
  273.9 0.6 slice_bitcast_fusion.7
  274.6 0.9 copy-done.4
  275.5 2.3 subtract_reduce_fusion.3
  278.0 0.6 slice_bitcast_fusion.10
  278.6 1.5 copy-done.1
  280.8 0.6 slice_bitcast_fusion.13
  281.4 3.5 %subtract_reduce_fusion.6 = (f32[2,32,2,128]{3,1,2,0:T(8,128)S(1)}, f32[2,32,2,128]{3,1,2,0:T(8,128)S(1)}, f32[2,32,2,128]{3,1,2,0:T(8,128)S(1)}, f32[2,32,2,128...) fusion(f32[32,2,32,2,128]{4,2,3,1,0:T(8,128)S(1)} %get-tuple-element.74, ...), kind=kLoop, calls=%fused_computation.14 | loop fusion | flops 25067520 | bytes 13107200 | tf_op jit(solution)/shard_map/reduce_sum | solution.py:44
  285.5 1.1 copy.98
  (70 shorter events, 5.4 us)
Async XLA Ops:
  6.5 101.4 %all-gather.6.cloned.1.call-start = ((), (), s32[]{:S(2)}) async-start(), calls=%async_computation.1 | async-start | bytes 4325376 | tf_op jit(solution)/shard_map/all_gather | solution.py:87
  12.9 1.3 copy-start
  21.9 167.8 %all-gather.8.cloned.1.call-start = ((), (), s32[]{:S(2)}) async-start(), calls=%async_computation.2 | async-start | bytes 4325376 | tf_op jit(solution)/shard_map/all_gather | solution.py:87
  31.9 239.0 %all-gather.4.cloned.1.call-start = ((), (), s32[]{:S(2)}) async-start(), calls=%async_computation | async-start | bytes 4325376 | tf_op jit(solution)/shard_map/all_gather | solution.py:87
  42.0 64.4 %collective-permute-start.2 = (f32[2,32,2,2,128]{4,3,2,1,0:T(2,128)S(1)}, f32[2,32,2,2,128]{4,3,2,1,0:T(2,128)S(1)}, u32[]{:S(2)}, u32[]{:S(2)}) collective-permute-start(f32[2,32,2,2,128]{4,3,2,1,0:T(2,128)S(1)} %reshape.374), channel_id=1, source_target_pairs={{32,0},{64,32},{96,64},{128,96},{160,128},{192,160},{224,192},{0,2... | collective-permute-start | bytes 393224 | tf_op jit(solution)/shard_map/ppermute | solution.py:85
  44.2 6.2 %copy-start.6 = (s32[1,3,32,16]{2,3,1,0:T(8,128)S(1)}, s32[1,3,32,16]{2,3,1,0:T(8,128)}, u32[]{:S(2)}) copy-start(s32[1,3,32,16]{2,3,1,0:T(8,128)} %param.10) | copy-start | bytes 18436
  44.2 62.2 %collective-permute-start = (f32[2,32,2,2,128]{4,3,2,1,0:T(2,128)S(1)}, f32[2,32,2,2,128]{4,3,2,1,0:T(2,128)S(1)}, u32[]{:S(2)}, u32[]{:S(2)}) collective-permute-start(f32[2,32,2,2,128]{4,3,2,1,0:T(2,128)S(1)} %reshape.373), channel_id=1, source_target_pairs={{0,32},{32,64},{64,96},{96,128},{128,160},{160,192},{192,224},{224... | collective-permute-start | bytes 393224 | tf_op jit(solution)/shard_map/ppermute | solution.py:83
  44.4 60.2 %copy-start.7 = (f32[8,2]{0,1:T(2,128)S(1)}, f32[8,2]{0,1:T(2,128)}, u32[]{:S(2)}) copy-start(f32[8,2]{0,1:T(2,128)} %param.11) | copy-start | bytes 196
  194.0 1.6 copy-start.5
  195.6 2.4 copy-start.3
  198.0 87.1 %collective-permute-start.3 = (f32[2,64,2,2,128]{4,1,2,0,3:T(8,128)S(1)}, f32[2,64,2,2,128]{4,1,2,0,3:T(8,128)S(1)}, u32[]{:S(2)}, u32[]{:S(2)}) collective-permute-start(f32[2,64,2,2,128]{4,1,2,0,3:T(8,128)S(1)} %maximum_maximum_fusion.2), channel_id=1, source_target_pairs={{0,32},{32,64},{64,96},{96,128},{128,160},{160,192},{192,224},{224... | collective-permute-start | bytes 786440 | tf_op jit(solution)/shard_map/ppermute | solution.py:100
  273.9 1.6 copy-start.4
  275.5 2.4 copy-start.2
  277.9 7.1 %collective-permute-start.1 = (f32[2,64,2,2,128]{4,1,2,0,3:T(8,128)S(1)}, f32[2,64,2,2,128]{4,1,2,0,3:T(8,128)S(1)}, u32[]{:S(2)}, u32[]{:S(2)}) collective-permute-start(f32[2,64,2,2,128]{4,1,2,0,3:T(8,128)S(1)} %maximum_maximum_fusion.1), channel_id=1, source_target_pairs={{32,0},{64,32},{96,64},{128,96},{160,128},{192,160},{224,192},{0,2... | collective-permute-start | bytes 786440 | tf_op jit(solution)/shard_map/ppermute | solution.py:99
  277.9 2.2 copy-start.1
Sparse Core Ops, SparseCore 0:
  22.0 85.9 all-gather.5
  110.6 79.0 all-gather.7
  192.3 78.5 all-gather.3
where the time goes:
time: 295 us; the launch traced here: 293 us
  waiting for transfers between devices  147 us (50%)
  blocking collectives  53.4 us (18%)
  local copies, waits for them, and re-layouts  28.4 us (10%)
  matrix products  24.6 us (8%)
  other arithmetic  23.7 us (8%)
  between operations  13.6 us (5%)
    all_gather x3, waiting for transfers between devices, body(): gathered = [lax.all_gather(t, 'grp', axis=0, tiled=False) for t in thirds]  147 us
    all_gather x1, blocking collectives, body(): lax.all_gather(taper_index.reshape(sides, group_count, CAP), 'grp', axis=...  53.4 us
    dot_general x3, matrix products, spectrum(): jnp.dot(traces.reshape(shots * recv, samples), table, precision=HIGHEST)  24.6 us
    mul x3, other arithmetic, combine(): gathered * jnp.transpose(weight, (0, 2, 1))[:, :, :, None, None, None]  13.1 us
    reduce_sum x3, other arithmetic, combine(): prod_re = -jnp.sum(col_re * row_re - col_im * row_im, axis=(1, 2))  8.05 us
    mul x7, local copies, waits for them, and re-layouts, combine(): prod_re = -jnp.sum(col_re * row_re - col_im * row_im, axis=(1, 2))  6.75 us
  transfers between devices with their start and end apart: 7, of which 3 were waited for; matrix products, arithmetic and copies ran while one was open for 19% of the time, Pallas kernels for 0%

commit v1 on v0

v1 whole, which is shorter than its diff:
```python
import math

import jax
import jax.numpy as jnp
import numpy as np
from jax import lax
from jax.sharding import Mesh, NamedSharding
from jax.sharding import PartitionSpec as P

NF = 128
BP = 2
CAP = 16
RADIX = 64

HIGHEST = lax.Precision.HIGHEST


def dft_matrix(samples):
    inner = samples // RADIX
    major = jnp.arange(RADIX, dtype=jnp.int32)
    minor = jnp.arange(inner, dtype=jnp.int32)
    bins = jnp.arange(NF, dtype=jnp.int32)
    step = 2.0 * math.pi / samples
    angle_a = ((major[:, None] * inner * bins[None, :]) % samples).astype(jnp.float32) * step
    angle_n = ((minor[:, None] * bins[None, :]) % samples).astype(jnp.float32) * step
    a_re, a_im = jnp.cos(angle_a), -jnp.sin(angle_a)
    n_re, n_im = jnp.cos(angle_n), -jnp.sin(angle_n)
    scale = 1.0 / math.sqrt(samples)
    c_re = (a_re[:, None, :] * n_re[None, :, :] - a_im[:, None, :] * n_im[None, :, :]) * scale
    c_im = (a_re[:, None, :] * n_im[None, :, :] + a_im[:, None, :] * n_re[None, :, :]) * scale
    return jnp.concatenate([c_re, c_im], axis=-1).reshape(samples, 2 * NF)


def spectrum(traces, table):
    shots, recv, samples = traces.shape
    out = jnp.dot(traces.reshape(shots * recv, samples), table, precision=HIGHEST)
    return out.reshape(shots, recv // BP, BP, 2, NF)


def combine(side_cols, weight, gathered):
    scaled = gathered[None] * jnp.transpose(weight, (0, 1, 3, 2))[:, :, :, :, None, None, None]
    col_re = side_cols[:, :, :, :, None, None, 0, :]
    col_im = side_cols[:, :, :, :, None, None, 1, :]
    row_re = scaled[:, None, :, :, :, :, 0, :]
    row_im = scaled[:, None, :, :, :, :, 1, :]
    prod_re = -jnp.sum(col_re * row_re - col_im * row_im, axis=(2, 3))
    prod_im = -jnp.sum(col_re * row_im + col_im * row_re, axis=(2, 3))
    return jnp.stack([prod_re, prod_im], axis=4)


def body(shot_traces, aperture, taper_index, taper_table):
    line_count = lax.axis_size("line")
    rows = lax.axis_size("gy")
    cols = lax.axis_size("gz")
    group_count = rows * cols
    my_line = lax.axis_index("line")
    my_row = lax.axis_index("gy")
    my_col = lax.axis_index("gz")
    shots, recv, samples = shot_traces.shape
    sides = 3
    width = recv // (BP * sides)
    up = [(i, (i + 1) % line_count) for i in range(line_count)]
    down = [((i + 1) % line_count, i) for i in range(line_count)]

    taper_rows = taper_table.shape[0]
    pick = taper_index.reshape(sides, rows, cols, CAP)[..., None] == jnp.arange(taper_rows, dtype=jnp.int32)
    src_weight = jnp.sum(jnp.where(pick[..., None], taper_table, 0.0), axis=-2)
    src_weight = lax.dynamic_index_in_dim(
        lax.all_gather(src_weight, "gz", axis=0, tiled=False), my_col, 3, False
    )
    full_table = aperture.reshape(line_count, rows, cols, sides, rows, cols, CAP)
    slot_list = lax.dynamic_index_in_dim(
        lax.dynamic_index_in_dim(
            lax.dynamic_index_in_dim(full_table, my_line, 0, False), my_row, 0, False
        ),
        my_col,
        3,
        False,
    )
    hit = slot_list[..., None] == jnp.arange(sides * width, dtype=jnp.int32)
    weight = jnp.sum(jnp.where(hit[..., None], src_weight[:, :, :, :, None, :], 0.0), axis=3)
    weight = jnp.transpose(weight, (1, 2, 0, 3, 4))

    table = dft_matrix(samples)
    thirds = [
        spectrum(lax.slice_in_dim(shot_traces, q * width * BP, (q + 1) * width * BP, axis=1), table)
        for q in range(sides)
    ]
    gathered = [lax.all_gather(t, "gz", axis=0, tiled=False) for t in thirds]

    stacked = jnp.stack(thirds).reshape(sides, shots, rows, cols, BP, 2, NF)
    spread = lax.all_to_all(stacked, "gy", split_axis=2, concat_axis=2, tiled=True)
    spread = jnp.transpose(spread, (0, 2, 1, 3, 4, 5, 6))
    side_cols = [
        lax.ppermute(spread[2], "line", up),
        spread[1],
        lax.ppermute(spread[0], "line", down),
    ]

    parts = {}
    for q in range(sides):
        for s in range(sides):
            if not 0 <= q + 1 - s < sides:
                continue
            w = weight[s, :, :, q * width:(q + 1) * width, :]
            local = combine(side_cols[s], w, gathered[q])
            parts[s, q] = lax.psum_scatter(local, "gy", scatter_dimension=0, tiled=False)

    to_down = jnp.concatenate([parts[0, 0], parts[0, 1]], axis=1)
    to_up = jnp.concatenate([parts[2, 1], parts[2, 2]], axis=1)
    from_up = lax.ppermute(to_down, "line", down)
    from_down = lax.ppermute(to_up, "line", up)
    result = jnp.concatenate([parts[1, q] for q in range(sides)], axis=1)
    result = result.at[:, width:].add(from_up)
    result = result.at[:, : 2 * width].add(from_down)
    return result.reshape(shots, recv, 2, NF)


def grid_shape(mesh):
    row = mesh.devices[0]
    try:
        ys = sorted({d.coords[1] for d in row})
        zs = sorted({d.coords[2] for d in row})
        if len(ys) * len(zs) == len(row):
            return len(ys), len(zs)
    except Exception:
        pass
    return 4, len(row) // 4


def solution(mesh):
    rows, cols = grid_shape(mesh)
    lines = mesh.devices.shape[0]
    fine = Mesh(np.asarray(mesh.devices).reshape(lines, rows, cols), ("line", "gy", "gz"))
    split = ("line", "gy", "gz")
    mapped = jax.shard_map(
        body,
        mesh=fine,
        in_specs=(P(split, None, None), P(), P(split, None, None, None), P()),
        out_specs=P(split, None, None, None),
        check_vma=False,
    )
    out_sharding = NamedSharding(mesh, P(("line", "grp"), None, None, None))
    return jax.jit(mapped, out_shardings=out_sharding)
```

time: 295 us -> 342 us (1.16); the launches traced: 293 us -> 336 us
  waiting for transfers between devices: 147 us -> 176 us
  blocking collectives: 53.4 us -> 30.1 us
  local copies, waits for them, and re-layouts: 28.4 us -> 50.8 us
  other arithmetic: 23.7 us -> 34.1 us
    reduce_scatter x0 -> x7, waiting for transfers between devices: none -> 150 us  [body(): lax.psum_scatter(local, 'gy', scatter_dimension=0, tiled=False)]
    all_gather x3, waiting for transfers between devices: 147 us -> 20.7 us  [body(): gathered = [lax.all_gather(t, 'gz', axis=0, tiled=False) for t in thirds]]
    all_gather x1, blocking collectives: 53.4 us -> 30.1 us  [body(): lax.all_gather(src_weight, 'gz', axis=0, tiled=False)]
    mul x7, local copies, waits for them, and re-layouts: 6.75 us -> 19 us  [combine(): prod_re = -jnp.sum(col_re * row_re - col_im * row_im, axis=(2, 3))]
    unnamed x17 -> x16, local copies, waits for them, and re-layouts: 5.11 us -> 13.8 us
    another operation x6 -> x17, local copies, waits for them, and re-layouts: 2.18 us -> 9.2 us  [the longest x7 5.93 us: combine(): return jnp.stack([prod_re, prod_im], axis=4)]
    reshape x4 -> x0, local copies, waits for them, and re-layouts: 5.28 us -> none  [the longest x1 5.07 us: body(): aperture.reshape(line_count, group_count, sides, group_count, CAP)]
    ppermute x2, waiting for transfers between devices: 0.01 us -> 4.91 us  [the longest x1 2.99 us: body(): lax.ppermute(spread[2], 'line', up)]
  transfers between devices with their start and end apart: 7 -> 15, of which waited for: 3 -> 9; matrix products, arithmetic and copies ran while one was open for 19% -> 27% of each run, Pallas kernels for 0% -> 0%
where the time goes in v1:
time: 342 us; the launch traced here: 336 us
  waiting for transfers between devices  176 us (51%)
  local copies, waits for them, and re-layouts  50.8 us (15%)
  other arithmetic  34.1 us (10%)
  blocking collectives  30.1 us (9%)
  matrix products  24.8 us (7%)
  between operations  14.5 us (4%)
  starting transfers between devices  5.77 us (2%)
    reduce_scatter x7, waiting for transfers between devices, body(): lax.psum_scatter(local, 'gy', scatter_dimension=0, tiled=False)  150 us
    all_gather x1, blocking collectives, body(): lax.all_gather(src_weight, 'gz', axis=0, tiled=False)  30.1 us
    dot_general x3, matrix products, spectrum(): jnp.dot(traces.reshape(shots * recv, samples), table, precision=HIGHEST)  24.8 us
    all_gather x3, waiting for transfers between devices, body(): gathered = [lax.all_gather(t, 'gz', axis=0, tiled=False) for t in thirds]  20.7 us
    mul x7, local copies, waits for them, and re-layouts, combine(): prod_re = -jnp.sum(col_re * row_re - col_im * row_im, axis=(2, 3))  19 us
    mul x3, other arithmetic, combine(): gathered[None]  14.1 us
    unnamed x16, local copies, waits for them, and re-layouts  13.8 us
    reduce_sum x3, other arithmetic, combine(): prod_re = -jnp.sum(col_re * row_re - col_im * row_im, axis=(2, 3))  12.7 us
  transfers between devices with their start and end apart: 15, of which 9 were waited for; matrix products, arithmetic and copies ran while one was open for 27% of the time, Pallas kernels for 0%

profile of v1, /device:TPU:32, one launch (start us, length us, event | category | flops | bytes accessed | tf_op | source)
XLA Modules:
  0.0 335.7 jit_solution(8182253121505555927)
XLA Ops:
  6.9 5.4 %fusion.25 = (f32[2,64,4096]{2,1,0:T(8,128)S(1)}, f32[2,64,4096]{2,1,0:T(8,128)}, f32[2,64,4096]{2,1,0:T(8,128)}) fusion(f32[2,192,4096]{2,1,0:T(8,128)} %param.8), kind=kLoop, calls=%fused_computation.115 | loop fusion | bytes 12582912 | tf_op jit(solution)/jit(body)/shard_map/slice | solution.py:86
  12.9 1.3 copy-done
  14.2 6.8 %fusion.4 = f32[128,256]{0,1:T(8,128)S(1)} fusion(f32[128,4096]{1,0:T(8,128)S(1)} %bitcast.134, f32[4096,128]{1,0:T(8,128)S(1)} %bitcast.128, f32[4096,128]{1,0:T(8,128)S(1)} %bitcast.125), kind=kOutput, calls=%fused_computation.43 | convolution fusion | flops 1611661312 | bytes 6422528 | tf_op jit(solution)/jit(body)/shard_map/dot_general | solution.py:36
  22.1 8.9 %fusion.3 = f32[128,256]{0,1:T(8,128)S(1)} fusion(f32[128,4096]{1,0:T(8,128)} %bitcast.133, f32[4096,128]{1,0:T(8,128)} %bitcast.129, f32[4096,128]{1,0:T(8,128)S(1)} %bitcast.126), kind=kOutput, calls=%fused_computation.42 | convolution fusion | flops 1611661312 | bytes 6422528 | tf_op jit(solution)/jit(body)/shard_map/dot_general | solution.py:36
  32.0 9.1 %fusion.5 = f32[128,256]{0,1:T(8,128)S(1)} fusion(f32[128,4096]{1,0:T(8,128)} %bitcast.132, f32[4096,128]{1,0:T(8,128)} %bitcast.130, f32[4096,128]{1,0:T(8,128)S(1)} %bitcast.127), kind=kOutput, calls=%fused_computation.44 | convolution fusion | flops 1611661312 | bytes 6422528 | tf_op jit(solution)/jit(body)/shard_map/dot_general | solution.py:36
  42.4 4.5 %all-to-all-start = ((f32[3,2,4,8,2,2,128]{6,5,4,3,1,0,2:T(2,128)}), f32[3,2,4,8,2,2,128]{6,5,4,3,1,0,2:T(2,128)S(1)}, u32[]{:S(2)}, u32[]{:S(2)}) async-start(f32[3,2,4,8,2,2,128]{6,5,4,3,1,0,2:T(2,128)} %copy.110), calls=%async_computation | async-start | bytes 786432 | tf_op jit(solution)/jit(body)/shard_map/all_to_all | solution.py:92
  47.7 10.5 %copy.114 = s32[256,3,32,16]{3,2,1,0:T(8,128)} copy(s32[256,3,32,16]{0,3,2,1:T(8,128)S(1)} %copy-done.4) | data formatting | bytes 3145728 | tf_op args[1]
  60.1 30.1 %all-gather = f32[24,4,8,16,2]{3,2,4,1,0:T(8,128)S(1)} all-gather(f32[3,4,8,16,2]{3,2,4,1,0:T(8,128)S(1)} %copy.118), channel_id=2, replica_groups=mesh['line'=8,'gy'=4,'gz'=8] {'gz'}, dimensions={0}, use_global_device_ids=true | all-gather | bytes 110592 | tf_op jit(solution)/jit(body)/shard_map/all_gather | solution.py:69
  92.1 1.9 collective-permute-done.2
  94.1 3.0 collective-permute-done
  97.3 6.2 %broadcast_multiply_fusion.1 = (f32[4,8,2,32,2,2,128]{6,3,4,2,1,0,5:T(8,128)}, f32[4,8,2,32,2,2,128]{6,3,4,2,1,0,5:T(8,128)S(1)}, f32[4,8,2,32,2,2,128]{6,3,4,2,1,0,5:T(8,128)}) fusion(f32[4,8,2,32]{3,2,0,1:T(2,128)S(1)} %get-tuple-element.91, f32[4,8,2,32]{3,2,0,1:T(2,128)S(1)} %get-tuple-element.88, ...), kind=kLoop, calls=%fused_computation.33 | loop fusion | flops 3145728 | bytes 13656064 | tf_op jit(solution)/jit(body)/shard_map/mul | solution.py:41
  103.5 2.0 slice_bitcast_fusion.4
  105.5 3.9 %broadcast_multiply_fusion.3 = (f32[4,8,2,32,2,2,128]{6,3,4,2,1,0,5:T(8,128)S(1)}, f32[4,8,2,32,2,2,128]{6,3,4,2,1,0,5:T(8,128)}) fusion(f32[4,8,2,32]{3,2,0,1:T(2,128)S(1)} %get-tuple-element.92, f32[8,2,32,2,2,128]{5,2,4,3,1,0:T(8,128)} %all-gather.5.cloned.1.call-done, f32[4,8,2,32]{3,2,0,1:T(2,128)S(1)} %get-tuple-element.89), kind=kLoop, calls=%fused_computation.35 | loop fusion | flops 2097152 | bytes 9453568 | tf_op jit(solution)/jit(body)/shard_map/mul | solution.py:41
  111.0 2.4 subtract_reduce_fusion.3
  115.3 4.2 %slice_bitcast_fusion.3 = (f32[4,8,2,32,2,128]{5,3,4,2,1,0:T(8,128)S(1)}, f32[4,8,2,32,2,128]{5,3,4,2,1,0:T(8,128)}) fusion(f32[4,8,2,32,2,2,128]{6,3,4,2,1,0,5:T(8,128)} %get-tuple-element.70), kind=kLoop, calls=%fused_computation.21 | loop fusion | bytes 8388608 | tf_op jit(solution)/jit(body)/shard_map/mul | solution.py:46
  119.6 20.6 %all-gather.9.cloned.1.call-done = f32[8,2,32,2,2,128]{5,2,4,3,1,0:T(8,128)} async-done(((f32[1,2,32,2,2,128]{5,2,4,3,1,0:T(8,128)}), f32[8,2,32,2,2,128]{5,2,4,3,1,0:T(8,128)}) %all-gather.9.cloned.1.call-update) | async-done | bytes 1048592 | tf_op jit(solution)/jit(body)/shard_map/all_gather | solution.py:89
  140.2 3.9 %broadcast_multiply_fusion = (f32[4,8,2,32,2,2,128]{6,3,4,2,1,0,5:T(8,128)S(1)}, f32[4,8,2,32,2,2,128]{6,3,4,2,1,0,5:T(8,128)}) fusion(f32[4,8,2,32]{3,2,0,1:T(2,128)S(1)} %get-tuple-element.90, f32[8,2,32,2,2,128]{5,2,4,3,1,0:T(8,128)} %all-gather.9.cloned.1.call-done, f32[4,8,2,32]{3,2,0,1:T(2,128)S(1)} %get-tuple-element.86), kind=kLoop, calls=%fused_computation.32 | loop fusion | flops 2097152 | bytes 9453568 | tf_op jit(solution)/jit(body)/shard_map/mul | solution.py:41
  144.2 2.5 slice_bitcast_fusion
  147.0 4.2 %subtract_reduce_fusion.1 = (f32[4,2,32,2,128]{4,2,3,1,0:T(8,128)S(1)}, f32[4,2,32,2,128]{4,2,3,1,0:T(8,128)S(1)}, f32[4,2,32,2,128]{4,2,3,1,0:T(8,128)S(1)}, f32[4,2,32,2,128]{4,2,3,1,0:T(8,128)S(1)}) fusion(f32[4,8,2,32,2,128]{5,3,4,2,1,0:T(8,128)} %get-tuple-element.57, f32[4,2,8,2,128]{4,3,2,1,0:T(2,128)S(1)} %bitcast.147, ...), kind=kLoop, calls=%fused_computation.4 | loop fusion | flops 16515072 | bytes 9568256 | tf_op jit(solution)/jit(body)/shard_map/reduce_sum | solution.py:46
  153.2 4.4 %slice_bitcast_fusion.10 = (f32[4,8,2,32,2,128]{5,3,4,2,1,0:T(8,128)S(1)}, f32[4,8,2,32,2,128]{5,3,4,2,1,0:T(8,128)}) fusion(f32[4,8,2,32,2,2,128]{6,3,4,2,1,0,5:T(8,128)} %get-tuple-element.72), kind=kLoop, calls=%fused_computation.28 | loop fusion | bytes 8388608 | tf_op jit(solution)/jit(body)/shard_map/mul | solution.py:46
  157.6 2.6 slice_bitcast_fusion.8
  160.2 1.1 copy-done.1
  161.3 2.4 slice_bitcast_fusion.13
  163.8 6.2 %subtract_reduce_fusion.6 = (f32[4,2,32,2,128]{4,2,3,1,0:T(8,128)S(1)}, f32[4,2,32,2,128]{4,2,3,1,0:T(8,128)S(1)}, f32[4,2,32,2,128]{4,2,3,1,0:T(8,128)S(1)}, f3...) fusion(f32[4,8,2,32,2,128]{5,3,4,2,1,0:T(8,128)} %get-tuple-element.67, ...), kind=kLoop, calls=%fused_computation.14 | loop fusion | flops 24772608 | bytes 14286848 | tf_op jit(solution)/jit(body)/shard_map/reduce_sum | solution.py:46
  173.0 19.2 %reduce-scatter.16.cloned.1.call-done = f32[1,2,32,2,2,128]{5,2,4,3,1,0:T(8,128)} async-done(((f32[4,2,32,2,2,128]{5,2,4,3,1,0:T(8,128)}), f32[1,2,32,2,2,128]{5,2,4,3,1,0:T(8,128)}) %reduce-scatter.16.cloned.1.call-update) | async-done | bytes 131088 | tf_op jit(solution)/jit(body)/shard_map/reduce_scatter | solution.py:107
  193.2 25.4 %reduce-scatter.18.cloned.1.call-done = f32[1,2,32,2,2,128]{5,2,4,3,1,0:T(8,128)} async-done(((f32[4,2,32,2,2,128]{5,2,4,3,1,0:T(8,128)}), f32[1,2,32,2,2,128]{5,2,4,3,1,0:T(8,128)}) %reduce-scatter.18.cloned.1.call-update) | async-done | bytes 131088 | tf_op jit(solution)/jit(body)/shard_map/reduce_scatter | solution.py:107
  218.6 26.6 %reduce-scatter.20.cloned.1.call-done = f32[1,2,32,2,2,128]{5,2,4,3,1,0:T(8,128)} async-done(((f32[4,2,32,2,2,128]{5,2,4,3,1,0:T(8,128)}), f32[1,2,32,2,2,128]{5,2,4,3,1,0:T(8,128)}) %reduce-scatter.20.cloned.1.call-update) | async-done | bytes 131088 | tf_op jit(solution)/jit(body)/shard_map/reduce_scatter | solution.py:107
  246.2 25.6 %reduce-scatter.8.cloned.1.call-done = f32[1,2,32,2,2,128]{5,2,4,3,1,0:T(8,128)} async-done(((f32[4,2,32,2,2,128]{5,2,4,3,1,0:T(8,128)}), f32[1,2,32,2,2,128]{5,2,4,3,1,0:T(8,128)}) %reduce-scatter.8.cloned.1.call-update) | async-done | bytes 131088 | tf_op jit(solution)/jit(body)/shard_map/reduce_scatter | solution.py:107
  271.8 26.6 %reduce-scatter.10.cloned.1.call-done = f32[1,2,32,2,2,128]{5,2,4,3,1,0:T(8,128)} async-done(((f32[4,2,32,2,2,128]{5,2,4,3,1,0:T(8,128)}), f32[1,2,32,2,2,128]{5,2,4,3,1,0:T(8,128)}) %reduce-scatter.10.cloned.1.call-update) | async-done | bytes 131088 | tf_op jit(solution)/jit(body)/shard_map/reduce_scatter | solution.py:107
  298.4 26.4 %reduce-scatter.12.cloned.1.call-done = f32[1,2,32,2,2,128]{5,2,4,3,1,0:T(8,128)} async-done(((f32[4,2,32,2,2,128]{5,2,4,3,1,0:T(8,128)}), f32[1,2,32,2,2,128]{5,2,4,3,1,0:T(8,128)}) %reduce-scatter.12.cloned.1.call-update) | async-done | bytes 131088 | tf_op jit(solution)/jit(body)/shard_map/reduce_scatter | solution.py:107
  324.9 1.1 pad_maximum_fusion.18
  327.4 1.1 copy.140
  (107 shorter events, 21.0 us)
Async XLA Ops:
  6.5 90.7 %all-gather.7.cloned.1.call-start = ((), (), s32[]{:S(2)}) async-start(), calls=%async_computation.10 | async-start | bytes 1179648 | tf_op jit(solution)/jit(body)/shard_map/all_gather | solution.py:89
  12.9 1.3 copy-start
  21.9 83.6 %all-gather.5.cloned.1.call-start = ((), (), s32[]{:S(2)}) async-start(), calls=%async_computation.8 | async-start | bytes 1179648 | tf_op jit(solution)/jit(body)/shard_map/all_gather | solution.py:89
  41.1 6.6 %copy-start.4 = (s32[256,3,32,16]{0,3,2,1:T(8,128)S(1)}, s32[256,3,32,16]{0,3,2,1:T(8,128)}, u32[]{:S(2)}) copy-start(s32[256,3,32,16]{0,3,2,1:T(8,128)} %param.9) | copy-start | bytes 4718596
  42.4 49.0 %all-to-all-start = ((f32[3,2,4,8,2,2,128]{6,5,4,3,1,0,2:T(2,128)}), f32[3,2,4,8,2,2,128]{6,5,4,3,1,0,2:T(2,128)S(1)}, u32[]{:S(2)}, u32[]{:S(2)}) async-start(f32[3,2,4,8,2,2,128]{6,5,4,3,1,0,2:T(2,128)} %copy.110), calls=%async_computation | async-start | bytes 786432 | tf_op jit(solution)/jit(body)/shard_map/all_to_all | solution.py:92
  46.8 93.4 %all-gather.9.cloned.1.call-start = ((), (), s32[]{:S(2)}) async-start(), calls=%async_computation.12 | async-start | bytes 1179648 | tf_op jit(solution)/jit(body)/shard_map/all_gather | solution.py:89
  47.6 125.4 %reduce-scatter.14.cloned.1.call-start = ((), (), s32[]{:S(2)}) async-start(), calls=%async_computation.14 | async-start | bytes 655360 | tf_op jit(solution)/jit(body)/shard_map/reduce_scatter | solution.py:107
  47.7 11.9 %copy-start.5 = (s32[1,3,32,16]{2,3,1,0:T(8,128)S(1)}, s32[1,3,32,16]{2,3,1,0:T(8,128)}, u32[]{:S(2)}) copy-start(s32[1,3,32,16]{2,3,1,0:T(8,128)} %param.10) | copy-start | bytes 18436
  47.7 12.0 %copy-start.6 = (f32[8,2]{0,1:T(2,128)S(1)}, f32[8,2]{0,1:T(2,128)}, u32[]{:S(2)}) copy-start(f32[8,2]{0,1:T(2,128)} %param.11) | copy-start | bytes 196
  91.5 2.5 collective-permute-start.2
  91.5 5.6 %collective-permute-start = (f32[4,2,8,2,2,128]{5,4,3,2,1,0:T(2,128)S(1)}, f32[4,2,8,2,2,128]{5,4,3,2,1,0:T(2,128)S(1)}, u32[]{:S(2)}, u32[]{:S(2)}) collective-permute-start(f32[4,2,8,2,2,128]{5,4,3,2,1,0:T(2,128)S(1)} %get-tuple-element.76), channel_id=1, source_target_pairs={{0,32},{32,64},{64,96},{96,128},{128,160},{160,192},{192,224},{224... | collective-permute-start | bytes 393224 | tf_op jit(solution)/jit(body)/shard_map/ppermute | solution.py:95
  109.4 1.6 copy-start.3
  115.3 76.9 %reduce-scatter.16.cloned.1.call-start = ((), (), s32[]{:S(2)}) async-start(), calls=%async_computation.15 | async-start | bytes 655360 | tf_op jit(solution)/jit(body)/shard_map/reduce_scatter | solution.py:107
  146.7 71.9 %reduce-scatter.18.cloned.1.call-start = ((), (), s32[]{:S(2)}) async-start(), calls=%async_computation.16 | async-start | bytes 655360 | tf_op jit(solution)/jit(body)/shard_map/reduce_scatter | solution.py:107
  153.1 92.1 %reduce-scatter.20.cloned.1.call-start = ((), (), s32[]{:S(2)}) async-start(), calls=%async_computation.17 | async-start | bytes 655360 | tf_op jit(solution)/jit(body)/shard_map/reduce_scatter | solution.py:107
  153.2 4.4 %copy-start.2 = (f32[4,8,2,32,2,2,128]{6,3,4,2,1,0,5:T(8,128)S(1)}, f32[4,8,2,32,2,2,128]{6,3,4,2,1,0,5:T(8,128)}, u32[]{:S(2)}) copy-start(f32[4,8,2,32,2,2,128]{6,3,4,2,1,0,5:T(8,128)} %get-tuple-element.69) | copy-start | bytes 12582916
  157.6 3.7 %copy-start.1 = (f32[4,8,2,32,2,2,128]{6,3,4,2,1,0,5:T(8,128)S(1)}, f32[4,8,2,32,2,2,128]{6,3,4,2,1,0,5:T(8,128)}, u32[]{:S(2)}) copy-start(f32[4,8,2,32,2,2,128]{6,3,4,2,1,0,5:T(8,128)} %get-tuple-element.74) | copy-start | bytes 12582916
  163.7 108.1 %reduce-scatter.8.cloned.1.call-start = ((), (), s32[]{:S(2)}) async-start(), calls=%async_computation.9 | async-start | bytes 655360 | tf_op jit(solution)/jit(body)/shard_map/reduce_scatter | solution.py:107
  171.0 127.5 %reduce-scatter.10.cloned.1.call-start = ((), (), s32[]{:S(2)}) async-start(), calls=%async_computation.11 | async-start | bytes 655360 | tf_op jit(solution)/jit(body)/shard_map/reduce_scatter | solution.py:107
  172.0 152.9 %reduce-scatter.12.cloned.1.call-start = ((), (), s32[]{:S(2)}) async-start(), calls=%async_computation.13 | async-start | bytes 655360 | tf_op jit(solution)/jit(body)/shard_map/reduce_scatter | solution.py:107
  193.2 132.7 %collective-permute-start.1 = (f32[2,64,2,2,128]{4,1,3,2,0:T(8,128)S(1)}, f32[2,64,2,2,128]{4,1,3,2,0:T(8,128)S(1)}, u32[]{:S(2)}, u32[]{:S(2)}) collective-permute-start(f32[2,64,2,2,128]{4,1,3,2,0:T(8,128)S(1)} %pad_maximum_fusion.19), channel_id=1, source_target_pairs={{32,0},{64,32},{96,64},{128,96},{160,128},{192,160},{224,192},{0,2... | collective-permute-start | bytes 786440 | tf_op jit(solution)/jit(body)/shard_map/ppermute | solution.py:111
  246.2 80.8 %collective-permute-start.3 = (f32[2,64,2,2,128]{4,1,3,2,0:T(8,128)S(1)}, f32[2,64,2,2,128]{4,1,3,2,0:T(8,128)S(1)}, u32[]{:S(2)}, u32[]{:S(2)}) collective-permute-start(f32[2,64,2,2,128]{4,1,3,2,0:T(8,128)S(1)} %pad_maximum_fusion.20), channel_id=1, source_target_pairs={{0,32},{32,64},{64,96},{96,128},{128,160},{160,192},{192,224},{224... | collective-permute-start | bytes 786440 | tf_op jit(solution)/jit(body)/shard_map/ppermute | solution.py:112
Sparse Core Ops, SparseCore 0:
  22.0 40.3 all-gather.6
  64.2 37.6 all-gather.4
  103.8 36.4 all-gather.8
  142.6 23.2 reduce-scatter.13
  168.2 23.9 reduce-scatter.15
  194.6 23.9 reduce-scatter.17
  221.1 24.0 reduce-scatter.19
  247.7 24.0 reduce-scatter.7
  274.4 24.0 reduce-scatter.9
  300.8 24.0 reduce-scatter.11
